TPU v7x, 128 devices: a whole 4x4x4 slice. The times are simulated.
128 devices in a mesh: ctx: 16 (over y, x), grp: 8 (over z, core).
Axes of the slice: x: 4, y: 4, z: 4, core: 2. Of those that a mesh axis runs over, the one named last changes fastest.
Arguments:
- residual: bfloat16 [8, 2048, 2880], P('grp', 'ctx'), may hold values from -3 to 3
- queries: bfloat16 [8, 2048, 2048], P('grp', 'ctx'), may hold values from -8 to 8
- stretch_kv: bfloat16 [8, 2048, 1024], P('grp', 'ctx'), may hold values from -8 to 8
- cache_kv: bfloat16 [8, 4096, 1024], P('grp', 'ctx'), may hold values from -6 to 6
- doc_lengths: int32 [8, 8], P('grp'), may hold values from 1 to 3072, 6144 in all within a row
- sinks: float32 [32], replicated, may hold values from 2 to 6
- out_proj: bfloat16 [2048, 2880], P('ctx'), may hold values from -0.75 to 0.75
- norm_gain: float32 [2880], replicated, may hold values from 0.1 to 1.9
- router: bfloat16 [2880, 64], replicated, may hold values from -0.109375 to 0.109375
- expert_ids: int32 [8, 2048, 4], P('grp', 'ctx'), may hold values from 0 to 63, all different within a row; in each aligned block of 128 rows (0 to 127, 128 to 255, ..., all dimensions but the last counted through in order) at most 10 rows name the same one
- expert_in: bfloat16 [128, 2880, 1536], P(('ctx', 'grp')), may hold values from -0.109375 to 0.109375
- expert_out: bfloat16 [128, 768, 2880], P(('ctx', 'grp')), may hold values from -0.15625 to 0.15625
Outputs:
- resid_mid: bfloat16 [8, 2048, 2880], P('grp', 'ctx')
- layer_out: bfloat16 [8, 2048, 2880], P('grp', 'ctx')
Inputs may be any that keep to these rules, and one draw needn't show every extreme that they name: `expert_ids`: in the rows of one device (aligned blocks of 128 tokens, sequence after sequence), each expert is named by at most 10 rows, and in some blocks one expert by exactly 10; a token's 4 experts differ. `doc_lengths`: A sequence's 8 lengths sum to 6144; the longest is exactly 3072.
All inputs are finite; a program needn't handle non-finite values.
Results may differ from a plain program's by a relative error of at most 0.015.
Values may be sent and summed in bfloat16 or wider, within the bound.
No kernel may reach another device: no remote copies, remote signals or barrier semaphores. Data moves between devices by JAX's collectives and lax.ppermute only.
A program may use at most 128 MiB of HBM per device.

v0:
```python
import math
import jax
import jax.numpy as jnp
from jax import lax
from jax.sharding import PartitionSpec as P

HEADS = 32
KVH = 8
HD = 64


def doc_index(positions, lengths):
    ends = jnp.cumsum(lengths)
    return jnp.sum((positions[:, None] >= ends[None, :]).astype(jnp.int32), axis=1)


def gated_act(pre, half_width):
    gate = pre[:, :half_width]
    upper = pre[:, half_width:]
    return ((upper + 1.0) * gate * jax.nn.sigmoid(1.702 * gate)).astype(jnp.bfloat16)


def body(
    residual,
    queries,
    stretch_kv,
    cache_kv,
    doc_lengths,
    sinks,
    out_proj,
    norm_gain,
    router,
    expert_ids,
    expert_in,
    expert_out,
):
    tokens = residual.shape[1]
    width = residual.shape[2]
    cache_rows = cache_kv.shape[1]
    kv_cols = stretch_kv.shape[2] // 2
    groups = HEADS // KVH
    ctx_count = lax.axis_size("ctx")
    ctx_here = lax.axis_index("ctx")
    stretch_base = cache_rows * ctx_count
    span = cache_rows + tokens
    query_pos = stretch_base + ctx_here * tokens + jnp.arange(tokens, dtype=jnp.int32)
    lengths = doc_lengths[0]
    query_doc = doc_index(query_pos, lengths)
    query_heads = queries[0].reshape(tokens, KVH, groups, HD)
    sink_grid = sinks.reshape(KVH, groups)
    local_kv = jnp.concatenate([cache_kv[0], stretch_kv[0]], axis=0)
    scale = 1.0 / math.sqrt(HD)

    def key_block(carry, keys_values, first):
        count = keys_values.shape[0]
        rows = first + jnp.arange(count, dtype=jnp.int32)
        source = rows // span
        offset = rows % span
        key_pos = jnp.where(
            offset < cache_rows,
            source * cache_rows + offset,
            stretch_base + source * tokens + offset - cache_rows,
        )
        key_doc = doc_index(key_pos, lengths)
        allowed = (key_pos[None, :] <= query_pos[:, None]) & (
            key_doc[None, :] == query_doc[:, None]
        )
        keys = keys_values[:, :kv_cols].reshape(count, KVH, HD)
        values = keys_values[:, kv_cols:].reshape(count, KVH, HD)
        top, total, numer = carry
        scores = (
            jnp.einsum("qkgd,skd->kgqs", query_heads, keys, preferred_element_type=jnp.float32)
            * scale
        )
        masked = jnp.where(allowed[None, None], scores, -jnp.inf)
        new_top = jnp.maximum(top, jnp.max(masked, axis=-1))
        weights = jnp.where(allowed[None, None], jnp.exp(scores - new_top[..., None]), 0.0)
        shrink = jnp.exp(top - new_top)
        total = total * shrink + jnp.sum(weights, axis=-1)
        numer = numer * shrink[..., None] + jnp.einsum(
            "kgqs,skd->kgqd",
            weights.astype(jnp.bfloat16),
            values,
            preferred_element_type=jnp.float32,
        )
        return (new_top, total, numer)

    start_top = jnp.broadcast_to(sink_grid[:, :, None], (KVH, groups, tokens))
    start_total = jnp.zeros((KVH, groups, tokens), jnp.float32)
    start_numer = jnp.zeros((KVH, groups, tokens, HD), jnp.float32)
    piece = lax.all_gather(local_kv, "ctx", axis=0, tiled=True)
    count = piece.shape[0]
    step_rows = math.gcd(count, 1024)

    def advance(index, state):
        first = index * step_rows
        part = lax.dynamic_slice_in_dim(piece, first, step_rows, 0)
        return key_block(state, part, first)

    top, total, numer = lax.fori_loop(
        0, count // step_rows, advance, (start_top, start_total, start_numer)
    )
    denom = total + jnp.exp(sink_grid[:, :, None] - top)
    attended = (
        jnp.transpose(numer / denom[..., None], (2, 0, 1, 3))
        .reshape(tokens, HEADS * HD)
        .astype(jnp.bfloat16)
    )
    projected = jnp.dot(
        attended,
        lax.all_gather(out_proj, "ctx", axis=0, tiled=True),
        preferred_element_type=jnp.float32,
    )
    mid = (residual[0].astype(jnp.float32) + projected).astype(jnp.bfloat16)
    mid_float = mid.astype(jnp.float32)
    normed = (
        mid_float
        * lax.rsqrt(jnp.mean(mid_float * mid_float, axis=-1, keepdims=True) + 1e-05)
        * norm_gain
    ).astype(jnp.bfloat16)
    logits = jnp.dot(normed, router, preferred_element_type=jnp.float32)
    experts = router.shape[1]
    chosen_ids = expert_ids[0]
    topk = chosen_ids.shape[1]
    picks = chosen_ids[:, :, None] == jnp.arange(experts, dtype=jnp.int32)[None, None, :]
    chosen = jnp.sum(jnp.where(picks, logits[:, None, :], 0.0), axis=-1)
    raised = jnp.exp(chosen)
    route_weights = raised / jnp.sum(raised, axis=-1, keepdims=True)
    capacity = 2 * ((5 * tokens * topk + 8 * experts - 1) // (8 * experts))
    flat_ids = chosen_ids.reshape(-1)
    pairs = flat_ids.shape[0]
    onehot = (flat_ids[:, None] == jnp.arange(experts, dtype=jnp.int32)[None, :]).astype(jnp.int32)
    slots = jnp.sum(onehot * (jnp.cumsum(onehot, axis=0) - 1), axis=1)
    dest = flat_ids * capacity + slots
    source_rows = jnp.arange(pairs, dtype=jnp.int32) // topk
    packed = jnp.zeros((experts * capacity, width), jnp.bfloat16).at[dest].set(normed[source_rows])
    packed = packed.reshape(experts, capacity, width)
    in_weights = expert_in[0]
    out_weights = expert_out[0]
    half_width = out_weights.shape[0]
    doubled = jnp.broadcast_to(packed[:, None], (experts, 2, capacity, width)).reshape(
        2 * experts, capacity, width
    )
    received = lax.all_to_all(doubled, ("ctx", "grp"), split_axis=0, concat_axis=0, tiled=True)
    flat_rows = received.reshape(-1, width)
    pre = jnp.dot(flat_rows, in_weights, preferred_element_type=jnp.float32)
    hidden = gated_act(pre, half_width)
    partial_out = jnp.dot(hidden, out_weights, preferred_element_type=jnp.float32).astype(
        jnp.bfloat16
    )
    partial_out = partial_out.reshape(received.shape)
    returned = lax.all_to_all(partial_out, ("ctx", "grp"), split_axis=0, concat_axis=0, tiled=True)
    pair_total = jnp.sum(returned.reshape(experts, 2, capacity, width).astype(jnp.float32), axis=1)
    expert_rows = pair_total.astype(jnp.bfloat16).reshape(experts * capacity, width)
    gathered = expert_rows[dest].astype(jnp.float32) * route_weights.reshape(-1)[:, None]
    mixture = jnp.sum(gathered.reshape(tokens, topk, width), axis=1)
    final = (mid_float + mixture).astype(jnp.bfloat16)
    return (mid[None], final[None])


def solution(mesh):
    return jax.shard_map(
        body,
        mesh=mesh,
        in_specs=(
            P("grp", "ctx", None),
            P("grp", "ctx", None),
            P("grp", "ctx", None),
            P("grp", "ctx", None),
            P("grp", None),
            P(),
            P("ctx", None),
            P(),
            P(),
            P("grp", "ctx", None),
            P(("ctx", "grp"), None, None),
            P(("ctx", "grp"), None, None),
        ),
        out_specs=(P("grp", "ctx", None), P("grp", "ctx", None)),
        check_vma=False,
    )
```

profile of v0, /device:TPU:66, one launch (start us, length us, event | category | flops | bytes accessed | tf_op | source)
XLA Modules:
  0.0 739.0 jit_solution(131095022201304216)
XLA Ops:
  14.6 97.2 %all-gather.3.cloned.1.call-done = bf16[6144,1024]{0,1:T(8,128)(2,1)} async-done(((bf16[384,1024]{0,1:T(8,128)(2,1)}), bf16[6144,1024]{0,1:T(8,128)(2,1)}) %all-gather.3.cloned.1.call-update) | async-done | bytes 12582928 | tf_op jit(solution)/shard_map/all_gather | solution.py:91
  111.8 157.7 %while.20 = (s32[]{:T(128)}, f32[8,4,128]{2,1,0:T(4,128)S(1)}, f32[8,4,128]{2,1,0:T(4,128)S(1)}, f32[8,4,128,64]{2,3,1,0:T(8,128)S(1)}, s32[1,8]{1,0:T(1,128)S(1...) while((s32[]{:T(128)}, f32[8,4,128]{2,1,0:T(4,128)S(1)}, ...), condition=%wide.region_7.8_spmd.clone, body=%wide.region_3.7_spmd.clone.sunk | while | flops 1121116288 | bytes 60053240 | solution.py:100
  114.0 7.1 fusion.69
  121.1 9.8 %fusion.70 = f32[8,4,128]{2,1,0:T(4,128)S(1)} fusion(f32[8,1024,128,4]{2,1,3,0:T(8,128)} %get-tuple-element.355, f32[8,4,128]{2,1,0:T(4,128)S(1)} %max.12, pred[128,1024]{0,1:T(8,128)(4,1)S(1)} %compare_and_fusion.2), kind=kLoop, calls=%fused_computation.10.clone.1 | loop fusion | flops 16773120 | bytes 16941056 | tf_op jit(solution)/shard_map/while/body/eval_jaxpr/reduce_sum | solution.py:79
  130.9 7.6 %fusion.72 = f32[8,4,128,64]{2,3,1,0:T(8,128)S(1)} fusion(bf16[1024,8,64,1]{0,2,3,1:T(8,128)(2,1)S(1)} %bitcast.98, f32[8,1024,128,4]{2,1,3,0:T(8,128)} %get-tuple-element.355, f32[8,4,128]{2,1,0:T(4,128)S(1)} %max.12, pred[128,1024]{0,1:T(8,128)(4,1)S(1)} %compare_and_fusion.2, f32[8,4,128,64]{2,3,1,0:T(8,128)S(1)} %get-tuple-element.376, ...), kind=kOutput, calls=%fused_computation.13.clone.1 | convolution fusion | flops 554434560 | bytes 20086784 | tf_op jit(solution)/shard_map/while/body/eval_jaxpr/kgqs,skd->kgqd/dot_general | solution.py:80
  140.9 7.1 fusion.69
  147.9 9.1 %fusion.70 = f32[8,4,128]{2,1,0:T(4,128)S(1)} fusion(f32[8,1024,128,4]{2,1,3,0:T(8,128)} %get-tuple-element.355, f32[8,4,128]{2,1,0:T(4,128)S(1)} %max.12, pred[128,1024]{0,1:T(8,128)(4,1)S(1)} %compare_and_fusion.2), kind=kLoop, calls=%fused_computation.10.clone.1 | loop fusion | flops 16773120 | bytes 16941056 | tf_op jit(solution)/shard_map/while/body/eval_jaxpr/reduce_sum | solution.py:79
  157.1 7.8 %fusion.72 = f32[8,4,128,64]{2,3,1,0:T(8,128)S(1)} fusion(bf16[1024,8,64,1]{0,2,3,1:T(8,128)(2,1)S(1)} %bitcast.98, f32[8,1024,128,4]{2,1,3,0:T(8,128)} %get-tuple-element.355, f32[8,4,128]{2,1,0:T(4,128)S(1)} %max.12, pred[128,1024]{0,1:T(8,128)(4,1)S(1)} %compare_and_fusion.2, f32[8,4,128,64]{2,3,1,0:T(8,128)S(1)} %get-tuple-element.376, ...), kind=kOutput, calls=%fused_computation.13.clone.1 | convolution fusion | flops 554434560 | bytes 20086784 | tf_op jit(solution)/shard_map/while/body/eval_jaxpr/kgqs,skd->kgqd/dot_general | solution.py:80
  167.1 7.2 fusion.69
  174.3 9.8 %fusion.70 = f32[8,4,128]{2,1,0:T(4,128)S(1)} fusion(f32[8,1024,128,4]{2,1,3,0:T(8,128)} %get-tuple-element.355, f32[8,4,128]{2,1,0:T(4,128)S(1)} %max.12, pred[128,1024]{0,1:T(8,128)(4,1)S(1)} %compare_and_fusion.2), kind=kLoop, calls=%fused_computation.10.clone.1 | loop fusion | flops 16773120 | bytes 16941056 | tf_op jit(solution)/shard_map/while/body/eval_jaxpr/reduce_sum | solution.py:79
  184.2 7.4 %fusion.72 = f32[8,4,128,64]{2,3,1,0:T(8,128)S(1)} fusion(bf16[1024,8,64,1]{0,2,3,1:T(8,128)(2,1)S(1)} %bitcast.98, f32[8,1024,128,4]{2,1,3,0:T(8,128)} %get-tuple-element.355, f32[8,4,128]{2,1,0:T(4,128)S(1)} %max.12, pred[128,1024]{0,1:T(8,128)(4,1)S(1)} %compare_and_fusion.2, f32[8,4,128,64]{2,3,1,0:T(8,128)S(1)} %get-tuple-element.376, ...), kind=kOutput, calls=%fused_computation.13.clone.1 | convolution fusion | flops 554434560 | bytes 20086784 | tf_op jit(solution)/shard_map/while/body/eval_jaxpr/kgqs,skd->kgqd/dot_general | solution.py:80
  193.9 7.2 fusion.69
  201.1 9.1 %fusion.70 = f32[8,4,128]{2,1,0:T(4,128)S(1)} fusion(f32[8,1024,128,4]{2,1,3,0:T(8,128)} %get-tuple-element.355, f32[8,4,128]{2,1,0:T(4,128)S(1)} %max.12, pred[128,1024]{0,1:T(8,128)(4,1)S(1)} %compare_and_fusion.2), kind=kLoop, calls=%fused_computation.10.clone.1 | loop fusion | flops 16773120 | bytes 16941056 | tf_op jit(solution)/shard_map/while/body/eval_jaxpr/reduce_sum | solution.py:79
  210.2 7.4 %fusion.72 = f32[8,4,128,64]{2,3,1,0:T(8,128)S(1)} fusion(bf16[1024,8,64,1]{0,2,3,1:T(8,128)(2,1)S(1)} %bitcast.98, f32[8,1024,128,4]{2,1,3,0:T(8,128)} %get-tuple-element.355, f32[8,4,128]{2,1,0:T(4,128)S(1)} %max.12, pred[128,1024]{0,1:T(8,128)(4,1)S(1)} %compare_and_fusion.2, f32[8,4,128,64]{2,3,1,0:T(8,128)S(1)} %get-tuple-element.376, ...), kind=kOutput, calls=%fused_computation.13.clone.1 | convolution fusion | flops 554434560 | bytes 20086784 | tf_op jit(solution)/shard_map/while/body/eval_jaxpr/kgqs,skd->kgqd/dot_general | solution.py:80
  226.9 9.1 %fusion.70 = f32[8,4,128]{2,1,0:T(4,128)S(1)} fusion(f32[8,1024,128,4]{2,1,3,0:T(8,128)} %get-tuple-element.355, f32[8,4,128]{2,1,0:T(4,128)S(1)} %max.12, pred[128,1024]{0,1:T(8,128)(4,1)S(1)} %compare_and_fusion.2), kind=kLoop, calls=%fused_computation.10.clone.1 | loop fusion | flops 16773120 | bytes 16941056 | tf_op jit(solution)/shard_map/while/body/eval_jaxpr/reduce_sum | solution.py:79
  236.1 7.4 %fusion.72 = f32[8,4,128,64]{2,3,1,0:T(8,128)S(1)} fusion(bf16[1024,8,64,1]{0,2,3,1:T(8,128)(2,1)S(1)} %bitcast.98, f32[8,1024,128,4]{2,1,3,0:T(8,128)} %get-tuple-element.355, f32[8,4,128]{2,1,0:T(4,128)S(1)} %max.12, pred[128,1024]{0,1:T(8,128)(4,1)S(1)} %compare_and_fusion.2, f32[8,4,128,64]{2,3,1,0:T(8,128)S(1)} %get-tuple-element.376, ...), kind=kOutput, calls=%fused_computation.13.clone.1 | convolution fusion | flops 554434560 | bytes 20086784 | tf_op jit(solution)/shard_map/while/body/eval_jaxpr/kgqs,skd->kgqd/dot_general | solution.py:80
  252.8 9.1 %fusion.70 = f32[8,4,128]{2,1,0:T(4,128)S(1)} fusion(f32[8,1024,128,4]{2,1,3,0:T(8,128)} %get-tuple-element.355, f32[8,4,128]{2,1,0:T(4,128)S(1)} %max.12, pred[128,1024]{0,1:T(8,128)(4,1)S(1)} %compare_and_fusion.2), kind=kLoop, calls=%fused_computation.10.clone.1 | loop fusion | flops 16773120 | bytes 16941056 | tf_op jit(solution)/shard_map/while/body/eval_jaxpr/reduce_sum | solution.py:79
  261.9 7.4 %fusion.72 = f32[8,4,128,64]{2,3,1,0:T(8,128)S(1)} fusion(bf16[1024,8,64,1]{0,2,3,1:T(8,128)(2,1)S(1)} %bitcast.98, f32[8,1024,128,4]{2,1,3,0:T(8,128)} %get-tuple-element.355, f32[8,4,128]{2,1,0:T(4,128)S(1)} %max.12, pred[128,1024]{0,1:T(8,128)(4,1)S(1)} %compare_and_fusion.2, f32[8,4,128,64]{2,3,1,0:T(8,128)S(1)} %get-tuple-element.376, ...), kind=kOutput, calls=%fused_computation.13.clone.1 | convolution fusion | flops 554434560 | bytes 20086784 | tf_op jit(solution)/shard_map/while/body/eval_jaxpr/kgqs,skd->kgqd/dot_general | solution.py:80
  269.7 7.7 %fusion.35 = (f32[128]{0:T(128)S(1)}, bf16[128,2880]{0,1:T(8,128)(2,1)S(1)}) fusion(bf16[2048,2880]{0,1:T(8,128)(2,1)} %all-gather.5.cloned.1.call-done, bf16[128,2048]{0,1:T(8,128)(2,1)S(1)} %bitcast.102, bf16[1,128,2880]{1,2,0:T(8,128)(2,1)} %param.14), kind=kOutput, calls=%fused_computation.55 | convolution fusion | flops 1512161152 | bytes 13795840 | tf_op jit(solution)/shard_map/dot_general | solution.py:109
  279.1 16.4 %scatter_custom_fusion = bf16[640,2880]{1,0:T(8,128)(2,1)} fusion(s32[512]{0:T(512)S(1)} %bitcast.106, bf16[128,2880]{1,0:T(8,128)(2,1)S(1)} %copy.54, s32[1024]{0:T(1024)S(1)} %pad_clamp_fusion.1, bf16[]{:T(256)} %constant.176.clone.1), kind=kCustom, calls=%fused_computation.47 | custom fusion | bytes 3686402 | tf_op jit(solution)/shard_map/scatter | solution.py:136
  295.6 7.3 broadcast_in_dim.138
  307.4 142.9 %all_to_all.10 = bf16[128,10,2880]{2,1,0:T(8,128)(2,1)} all-to-all(bf16[128,10,2880]{2,1,0:T(8,128)(2,1)S(1)} %bitcast.97), channel_id=1, replica_groups=mesh['ctx'=16,'grp'=8] {'ctx','grp'}, dimensions={0} | all-to-all | bytes 14745600 | tf_op jit(solution)/shard_map/all_to_all | solution.py:144
  450.2 14.4 %reshape.320 = bf16[1280,2880]{1,0:T(8,128)(2,1)} reshape(bf16[128,10,2880]{2,1,0:T(8,128)(2,1)} %all_to_all.10) | data formatting | bytes 14745600 | tf_op jit(solution)/shard_map/reshape | solution.py:145
  464.6 17.2 %fusion.22 = f32[1280,1536]{1,0:T(8,128)S(1)} fusion(bf16[1280,2880]{1,0:T(8,128)(2,1)} %reshape.320, bf16[1,2880,1536]{2,1,0:T(8,128)(2,1)} %param.24), kind=kOutput, calls=%fused_computation.37 | convolution fusion | flops 11324620800 | bytes 24084480 | tf_op jit(solution)/shard_map/dot_general | solution.py:146
  481.9 11.8 %convolution_convert_fusion = bf16[1280,2880]{0,1:T(8,128)(2,1)} fusion(bf16[1,768,2880]{1,2,0:T(8,128)(2,1)} %param.25, f32[1280,1536]{1,0:T(8,128)S(1)} %fusion.22), kind=kOutput, calls=%fused_computation.36 | convolution fusion | flops 5673861120 | bytes 19660800 | tf_op jit(solution)/shard_map/dot_general | solution.py:148
  493.6 10.4 %copy.55 = bf16[1280,2880]{1,0:T(8,128)(2,1)} copy(bf16[1280,2880]{0,1:T(8,128)(2,1)} %convolution_convert_fusion) | data formatting | bytes 14745600 | tf_op jit(solution)/shard_map/convert_element_type | solution.py:148
  504.1 13.4 %reshape.321 = bf16[128,10,2880]{2,1,0:T(8,128)(2,1)} reshape(bf16[1280,2880]{1,0:T(8,128)(2,1)} %copy.55) | data formatting | bytes 14745600 | tf_op jit(solution)/shard_map/reshape | solution.py:151
  517.5 12.0 %all-to-all-start.1 = ((bf16[128,10,2880]{2,1,0:T(8,128)(2,1)}), bf16[128,10,2880]{2,1,0:T(8,128)(2,1)}, u32[]{:S(2)}, u32[]{:S(2)}) async-start(bf16[128,10,2880]{2,1,0:T(8,128)(2,1)} %reshape.321), calls=%async_computation.1 | async-start | bytes 24117248 | tf_op jit(solution)/shard_map/all_to_all | solution.py:152
  530.0 157.7 %all-to-all-done.1 = bf16[128,10,2880]{2,1,0:T(8,128)(2,1)} async-done(((bf16[128,10,2880]{2,1,0:T(8,128)(2,1)}), bf16[128,10,2880]{2,1,0:T(8,128)(2,1)}, u32[]{:S(2)}, u32[]{:S(2)}) %all-to-all-start.1) | async-done | bytes 7372832 | tf_op jit(solution)/shard_map/all_to_all | solution.py:152
  687.7 14.7 %bitcast_reduce_fusion = bf16[64,10,2880]{2,1,0:T(8,128)(2,1)} fusion(bf16[128,10,2880]{2,1,0:T(8,128)(2,1)} %all-to-all-done.1), kind=kLoop, calls=%fused_computation.35 | loop fusion | flops 1843200 | bytes 11059200 | tf_op jit(solution)/shard_map/reduce_sum | solution.py:153
  702.4 7.8 %reshape.323 = bf16[640,2880]{1,0:T(8,128)(2,1)} reshape(bf16[64,10,2880]{2,1,0:T(8,128)(2,1)} %bitcast_reduce_fusion) | data formatting | bytes 7372800 | tf_op jit(solution)/shard_map/reshape | solution.py:154
  710.2 8.4 %gather_fusion = bf16[512,2880]{1,0:T(8,128)(2,1)S(1)} fusion(bf16[640,2880]{1,0:T(8,128)(2,1)} %reshape.323, s32[1024]{0:T(1024)S(1)} %pad_clamp_fusion), kind=kCustom, calls=%fused_computation.1 | custom fusion | bytes 5900288 | tf_op jit(solution)/shard_map/gather | solution.py:155
  (114 shorter events, 54.9 us)
Async XLA Ops:
  7.2 522.4 %copy-start = (bf16[2880,64]{0,1:T(8,128)(2,1)S(1)}, bf16[2880,64]{0,1:T(8,128)(2,1)}, u32[]{:S(2)}) copy-start(bf16[2880,64]{0,1:T(8,128)(2,1)} %param.22) | copy-start | bytes 1105924
  7.2 4.3 copy-start.3
  7.2 4.7 copy-start.6
  7.2 4.8 copy-start.7
  7.2 5.1 copy-start.2
  7.2 104.5 %all-gather.3.cloned.1.call-start = ((), (), s32[]{:S(2)}) async-start(), calls=%async_computation.2 | async-start | bytes 13369344 | tf_op jit(solution)/shard_map/all_gather | solution.py:91
  10.7 259.0 %all-gather.5.cloned.1.call-start = ((), (), s32[]{:S(2)}) async-start(), calls=%async_computation.3 | async-start | bytes 12533760 | tf_op jit(solution)/shard_map/all_gather | solution.py:111
  269.7 8.6 %copy-start.5 = (f32[2880]{0:T(1024)S(1)}, f32[2880]{0:T(1024)}, u32[]{:S(2)}) copy-start(f32[2880]{0:T(1024)} %param.21) | copy-start | bytes 34564
  277.5 0.9 copy-start.1
  517.5 12.3 %copy-start.4 = (s32[1,128,4]{1,2,0:T(4,128)S(1)}, s32[1,128,4]{1,2,0:T(4,128)}, u32[]{:S(2)}) copy-start(s32[1,128,4]{1,2,0:T(4,128)} %param.23) | copy-start | bytes 6148
  517.5 170.2 %all-to-all-start.1 = ((bf16[128,10,2880]{2,1,0:T(8,128)(2,1)}), bf16[128,10,2880]{2,1,0:T(8,128)(2,1)}, u32[]{:S(2)}, u32[]{:S(2)}) async-start(bf16[128,10,2880]{2,1,0:T(8,128)(2,1)} %reshape.321), calls=%async_computation.1 | async-start | bytes 24117248 | tf_op jit(solution)/shard_map/all_to_all | solution.py:152
Sparse Core Ops, SparseCore 0:
  10.8 100.8 all-gather.2
  113.8 94.9 all-gather.4
where the time goes:
time: 747 us; the launch traced here: 739 us
  waiting for transfers between devices  256 us (34%)
  blocking collectives  143 us (19%)
  matrix products  125 us (17%)
  local copies, waits for them, and re-layouts  102 us (14%)
  other arithmetic  86.3 us (12%)
  between operations  14.6 us (2%)
  starting transfers between devices  12.1 us (2%)
    all_to_all x1, waiting for transfers between devices, body(): lax.all_to_all(partial_out, ('ctx', 'grp'), split_axis=0, concat_axis=0,...  158 us
    all_to_all x1, blocking collectives, body(): lax.all_to_all(doubled, ('ctx', 'grp'), split_axis=0, concat_axis=0, tile...  143 us
    all_gather x1, waiting for transfers between devices, body(): piece = lax.all_gather(local_kv, 'ctx', axis=0, tiled=True)  97.2 us
    reduce_sum x6, other arithmetic, key_block(): total = total * shrink + jnp.sum(weights, axis=-1)  56 us
    dot_general x6, matrix products, key_block(): jnp.einsum('kgqs,skd->kgqd', weights.astype(jnp.bfloat16), values, prefer...  45 us
    dot_general x6, matrix products, key_block(): jnp.einsum('qkgd,skd->kgqs', query_heads, keys, preferred_element_type=jn...  42.7 us
    dot_general x1, matrix products, body(): pre = jnp.dot(flat_rows, in_weights, preferred_element_type=jnp.float32)  17.2 us
    scatter x1, local copies, waits for them, and re-layouts, body(): jnp.zeros((experts * capacity, width), jnp.bfloat16).at[dest]  16.4 us
  transfers between devices with their start and end apart: 3, of which 2 were waited for; matrix products, arithmetic and copies ran while one was open for 22% of the time, Pallas kernels for 0%

commit v1 on v0

--- a/solution.py
+++ b/solution.py
@@ -7,6 +7,11 @@
 HEADS = 32
 KVH = 8
 HD = 64
+
+
+def gather_by_exchange(x, axis, dim):
+    copies = jnp.concatenate([x] * lax.axis_size(axis), axis=dim)
+    return lax.all_to_all(copies, axis, dim, dim, tiled=True)
 
 
 def doc_index(positions, lengths):
@@ -88,7 +93,7 @@
     start_top = jnp.broadcast_to(sink_grid[:, :, None], (KVH, groups, tokens))
     start_total = jnp.zeros((KVH, groups, tokens), jnp.float32)
     start_numer = jnp.zeros((KVH, groups, tokens, HD), jnp.float32)
-    piece = lax.all_gather(local_kv, "ctx", axis=0, tiled=True)
+    piece = gather_by_exchange(local_kv, "ctx", 0)
     count = piece.shape[0]
     step_rows = math.gcd(count, 1024)
 

time: 747 us -> 951 us (1.27)
  waiting for transfers between devices: 256 us -> 349 us
  local copies, waits for them, and re-layouts: 102 us -> 162 us
  blocking collectives: 143 us -> 159 us
  matrix products: 125 us -> 138 us
  other arithmetic: 86.3 us -> 96.6 us
    all_to_all x0 -> x1, waiting for transfers between devices: none -> 190 us  [gather_by_exchange(): return lax.all_to_all(copies, axis, dim, dim, tiled=True)]
    all_gather x1 -> x0, waiting for transfers between devices: 97.2 us -> none  [body(): piece = lax.all_gather(local_kv, 'ctx', axis=0, tiled=True)]
    all_to_all x0 -> x2, local copies, waits for them, and re-layouts: none -> 33.3 us  [gather_by_exchange(): return lax.all_to_all(copies, axis, dim, dim, tiled=True)]
    unnamed x20 -> x59, local copies, waits for them, and re-layouts: 3.72 us -> 23.5 us
    all_to_all x1, blocking collectives: 143 us -> 159 us  [body(): lax.all_to_all(doubled, ('ctx', 'grp'), split_axis=0, concat_axis=0, tile...]
where the time goes in v1:
time: 951 us; the launch traced here: 939 us
  waiting for transfers between devices  349 us (37%)
  local copies, waits for them, and re-layouts  162 us (17%)
  blocking collectives  159 us (17%)
  matrix products  138 us (15%)
  other arithmetic  96.6 us (10%)
  starting transfers between devices  19.7 us (2%)
  between operations  14.7 us (2%)
    all_to_all x1, waiting for transfers between devices, gather_by_exchange(): return lax.all_to_all(copies, axis, dim, dim, tiled=True)  190 us
    all_to_all x1, blocking collectives, body(): lax.all_to_all(doubled, ('ctx', 'grp'), split_axis=0, concat_axis=0, tile...  159 us
    all_to_all x1, waiting for transfers between devices, body(): lax.all_to_all(partial_out, ('ctx', 'grp'), split_axis=0, concat_axis=0,...  158 us
    reduce_sum x6, other arithmetic, key_block(): total = total * shrink + jnp.sum(weights, axis=-1)  55 us
    dot_general x6, matrix products, key_block(): jnp.einsum('kgqs,skd->kgqd', weights.astype(jnp.bfloat16), values, prefer...  52.2 us
    dot_general x6, matrix products, key_block(): jnp.einsum('qkgd,skd->kgqs', query_heads, keys, preferred_element_type=jn...  48.9 us
    all_to_all x2, local copies, waits for them, and re-layouts, gather_by_exchange(): return lax.all_to_all(copies, axis, dim, dim, tiled=True)  33.3 us
    unnamed x59, local copies, waits for them, and re-layouts  23.5 us
  transfers between devices with their start and end apart: 3, of which 2 were waited for; matrix products, arithmetic and copies ran while one was open for 22% of the time, Pallas kernels for 0%

profile of v1, /device:TPU:66, one launch (start us, length us, event | category | flops | bytes accessed | tf_op | source)
XLA Modules:
  0.0 938.9 jit_solution(1563188771451900666)
XLA Ops:
  28.9 16.6 %copy.57 = bf16[16,384,1024]{1,2,0:T(8,128)(2,1)} copy(bf16[16,384,1024]{2,1,0:T(8,128)(2,1)} %bitcast.134) | data formatting | bytes 25165824 | tf_op jit(solution)/shard_map/all_to_all | solution.py:14
  60.0 190.1 %all-to-all-done = bf16[16,384,1024]{1,2,0:T(8,128)(2,1)} async-done(((bf16[16,384,1024]{1,2,0:T(8,128)(2,1)}), bf16[16,384,1024]{1,2,0:T(8,128)(2,1)}, u32[]{:S(2)}, u32[]{:S(2)}) %all-to-all-start) | async-done | bytes 12582944 | tf_op jit(solution)/shard_map/all_to_all | solution.py:14
  250.1 16.7 %copy.58 = bf16[16,384,1024]{2,1,0:T(8,128)(2,1)} copy(bf16[16,384,1024]{1,2,0:T(8,128)(2,1)} %all-to-all-done) | data formatting | bytes 25165824 | tf_op jit(solution)/shard_map/all_to_all | solution.py:14
  266.9 184.1 %while.20 = (s32[]{:T(128)}, f32[8,4,128]{2,1,0:T(4,128)S(1)}, f32[8,4,128]{2,1,0:T(4,128)S(1)}, f32[8,4,128,64]{2,3,1,0:T(8,128)}, s32[1,8]{1,0:T(1,128)}, /*in...) while((s32[]{:T(128)}, f32[8,4,128]{2,1,0:T(4,128)S(1)}, ...), condition=%wide.region_7.8_spmd.clone, body=%wide.region_3.7_spmd.clone.sunk | while | flops 1121116288 | bytes 64247544 | solution.py:105
  270.9 8.4 fusion.69
  279.3 9.5 %fusion.70 = f32[8,4,128]{2,1,0:T(4,128)S(1)} fusion(f32[8,1024,128,4]{2,1,3,0:T(8,128)} %get-tuple-element.373, f32[8,4,128]{2,1,0:T(4,128)S(1)} %max.12, pred[128,1024]{0,1:T(8,128)(4,1)S(1)} %compare_and_fusion.2), kind=kLoop, calls=%fused_computation.10.clone.1 | loop fusion | flops 16773120 | bytes 16941056 | tf_op jit(solution)/shard_map/while/body/eval_jaxpr/reduce_sum | solution.py:84
  289.4 8.5 fusion.72
  301.9 8.1 fusion.69
  310.1 9.1 fusion.70
  319.7 8.8 fusion.72
  332.5 8.1 fusion.69
  340.6 9.1 fusion.70
  350.3 8.8 fusion.72
  363.1 8.1 fusion.69
  371.2 9.1 fusion.70
  380.9 8.8 fusion.72
  401.8 9.1 fusion.70
  411.5 8.8 fusion.72
  424.3 8.1 fusion.69
  432.4 9.1 fusion.70
  442.1 8.8 fusion.72
  462.6 16.6 %scatter_custom_fusion = bf16[640,2880]{1,0:T(8,128)(2,1)} fusion(s32[512]{0:T(512)S(1)} %bitcast.140, bf16[128,2880]{1,0:T(8,128)(2,1)S(1)} %copy.65, s32[1024]{0:T(1024)} %pad_clamp_fusion.1, bf16[]{:T(256)} %constant.176.clone.1), kind=kCustom, calls=%fused_computation.47 | custom fusion | bytes 3686912 | tf_op jit(solution)/shard_map/scatter | solution.py:141
  490.9 159.2 %all_to_all.22 = bf16[128,10,2880]{2,1,0:T(8,128)(2,1)} all-to-all(bf16[128,10,2880]{2,1,0:T(8,128)(2,1)S(1)} %bitcast.131), channel_id=1, replica_groups=mesh['ctx'=16,'grp'=8] {'ctx','grp'}, dimensions={0} | all-to-all | bytes 14745600 | tf_op jit(solution)/shard_map/all_to_all | solution.py:149
  650.1 14.4 %reshape.322 = bf16[1280,2880]{1,0:T(8,128)(2,1)} reshape(bf16[128,10,2880]{2,1,0:T(8,128)(2,1)} %all_to_all.22) | data formatting | bytes 14745600 | tf_op jit(solution)/shard_map/reshape | solution.py:150
  664.5 17.2 %fusion.22 = f32[1280,1536]{1,0:T(8,128)S(1)} fusion(bf16[1280,2880]{1,0:T(8,128)(2,1)} %reshape.322, bf16[1,2880,1536]{2,1,0:T(8,128)(2,1)} %param.24), kind=kOutput, calls=%fused_computation.37 | convolution fusion | flops 11324620800 | bytes 24084480 | tf_op jit(solution)/shard_map/dot_general | solution.py:151
  681.8 11.8 %convolution_convert_fusion = bf16[1280,2880]{0,1:T(8,128)(2,1)} fusion(bf16[1,768,2880]{1,2,0:T(8,128)(2,1)} %param.25, f32[1280,1536]{1,0:T(8,128)S(1)} %fusion.22), kind=kOutput, calls=%fused_computation.36 | convolution fusion | flops 5673861120 | bytes 19660800 | tf_op jit(solution)/shard_map/dot_general | solution.py:153
  693.5 10.4 %copy.66 = bf16[1280,2880]{1,0:T(8,128)(2,1)} copy(bf16[1280,2880]{0,1:T(8,128)(2,1)} %convolution_convert_fusion) | data formatting | bytes 14745600 | tf_op jit(solution)/shard_map/convert_element_type | solution.py:153
  703.9 13.4 %reshape.323 = bf16[128,10,2880]{2,1,0:T(8,128)(2,1)} reshape(bf16[1280,2880]{1,0:T(8,128)(2,1)} %copy.66) | data formatting | bytes 14745600 | tf_op jit(solution)/shard_map/reshape | solution.py:156
  717.3 12.0 %all-to-all-start.2 = ((bf16[128,10,2880]{2,1,0:T(8,128)(2,1)}), bf16[128,10,2880]{2,1,0:T(8,128)(2,1)}, u32[]{:S(2)}, u32[]{:S(2)}) async-start(bf16[128,10,2880]{2,1,0:T(8,128)(2,1)} %reshape.323), calls=%async_computation.2 | async-start | bytes 24117248 | tf_op jit(solution)/shard_map/all_to_all | solution.py:157
  729.9 157.7 %all-to-all-done.2 = bf16[128,10,2880]{2,1,0:T(8,128)(2,1)} async-done(((bf16[128,10,2880]{2,1,0:T(8,128)(2,1)}), bf16[128,10,2880]{2,1,0:T(8,128)(2,1)}, u32[]{:S(2)}, u32[]{:S(2)}) %all-to-all-start.2) | async-done | bytes 7372832 | tf_op jit(solution)/shard_map/all_to_all | solution.py:157
  887.6 14.7 %bitcast_reduce_fusion = bf16[64,10,2880]{2,1,0:T(8,128)(2,1)} fusion(bf16[128,10,2880]{2,1,0:T(8,128)(2,1)} %all-to-all-done.2), kind=kLoop, calls=%fused_computation.35 | loop fusion | flops 1843200 | bytes 11059200 | tf_op jit(solution)/shard_map/reduce_sum | solution.py:158
  910.0 8.4 gather_fusion
  (166 shorter events, 116.4 us)
Async XLA Ops:
  7.2 722.2 %copy-start = (bf16[2880,64]{0,1:T(8,128)(2,1)S(1)}, bf16[2880,64]{0,1:T(8,128)(2,1)}, u32[]{:S(2)}) copy-start(bf16[2880,64]{0,1:T(8,128)(2,1)} %param.22) | copy-start | bytes 1105924
  7.2 16.6 %copy-start.1 = (bf16[1,256,1024]{2,1,0:T(8,128)(2,1)S(1)}, bf16[1,256,1024]{2,1,0:T(8,128)(2,1)}, u32[]{:S(2)}) copy-start(bf16[1,256,1024]{2,1,0:T(8,128)(2,1)} %param.17) | copy-start | bytes 1572868
  7.2 16.6 %copy-start.2 = (bf16[1,128,1024]{2,1,0:T(8,128)(2,1)S(1)}, bf16[1,128,1024]{2,1,0:T(8,128)(2,1)}, u32[]{:S(2)}) copy-start(bf16[1,128,1024]{2,1,0:T(8,128)(2,1)} %param.16) | copy-start | bytes 786436
  24.3 4.6 copy-start.3
  45.5 8.4 copy-start.7
  45.5 8.7 copy-start.11
  45.5 8.8 copy-start.12
  45.5 9.8 %copy-start.5 = (bf16[1,128,2048]{2,1,0:T(8,128)(2,1)S(1)}, bf16[1,128,2048]{2,1,0:T(8,128)(2,1)}, u32[]{:S(2)}) copy-start(bf16[1,128,2048]{2,1,0:T(8,128)(2,1)} %param.15) | copy-start | bytes 1572868
  45.5 204.6 %all-to-all-start = ((bf16[16,384,1024]{1,2,0:T(8,128)(2,1)}), bf16[16,384,1024]{1,2,0:T(8,128)(2,1)}, u32[]{:S(2)}, u32[]{:S(2)}) async-start(bf16[16,384,1024]{1,2,0:T(8,128)(2,1)} %copy.57), calls=%async_computation | async-start | bytes 25165824 | tf_op jit(solution)/shard_map/all_to_all | solution.py:14
  53.2 400.0 %all-gather.2.cloned.1.call-start = ((), (), s32[]{:S(2)}) async-start(), calls=%async_computation.3 | async-start | bytes 12533760 | tf_op jit(solution)/shard_map/all_gather | solution.py:116
  54.3 212.5 %copy-start.6 = (f32[8,4]{1,0:T(8,128)}, f32[8,4]{1,0:T(8,128)S(1)}, u32[]{:S(2)}) copy-start(f32[8,4]{1,0:T(8,128)S(1)} %broadcast_in_dim.131) | copy-start | bytes 388
  451.0 10.8 %copy-start.9 = (f32[2880]{0:T(1024)S(1)}, f32[2880]{0:T(1024)}, u32[]{:S(2)}) copy-start(f32[2880]{0:T(1024)} %param.21) | copy-start | bytes 34564
  451.0 11.6 %copy-start.10 = (s32[512,1]{0,1:T(1,128)S(1)}, s32[512,1]{0,1:T(1,128)}, u32[]{:S(2)}) copy-start(s32[512,1]{0,1:T(1,128)} %compare_select_fusion.1) | copy-start | bytes 6148
  460.9 0.9 copy-start.4
  717.3 12.3 %copy-start.8 = (s32[1,128,4]{1,2,0:T(4,128)S(1)}, s32[1,128,4]{1,2,0:T(4,128)}, u32[]{:S(2)}) copy-start(s32[1,128,4]{1,2,0:T(4,128)} %param.23) | copy-start | bytes 6148
  717.3 170.2 %all-to-all-start.2 = ((bf16[128,10,2880]{2,1,0:T(8,128)(2,1)}), bf16[128,10,2880]{2,1,0:T(8,128)(2,1)}, u32[]{:S(2)}, u32[]{:S(2)}) async-start(bf16[128,10,2880]{2,1,0:T(8,128)(2,1)} %reshape.323), calls=%async_computation.2 | async-start | bytes 24117248 | tf_op jit(solution)/shard_map/all_to_all | solution.py:157
Sparse Core Ops, SparseCore 0:
  56.1 243.3 all-gather.1
